TPU v7x, 128 devices: a whole 4x4x4 slice. The times are simulated.
128 devices in a mesh: req: 8 (over x, core), seq: 16 (over z, y).
Axes of the slice: x: 4, y: 4, z: 4, core: 2. Of those that a mesh axis runs over, the one named last changes fastest.
Arguments:
- hidden: bfloat16 [8, 2048, 2048], P('req', 'seq'), may hold values from -6 to 6
- lengths: int32 [8], replicated, may hold values from 1 to 2048, 10240 in all
- slot_request: int32 [8], replicated, may hold values from 0 to 7, each once
- norm_gain: bfloat16 [2048], replicated, may hold values from 0.099609375 to 1.8984375
- in_weight: bfloat16 [2, 2048, 4096], P(None, 'req', 'seq'), may hold values from -0.125 to 0.125
- conv_weight: bfloat16 [4, 4096], P(None, 'seq'), may hold values from -3 to 3
- conv_bias: bfloat16 [4096], P('seq'), may hold values from -0.5 to 0.5
- xproj_weight: bfloat16 [4096, 160], P('seq'), may hold values from -0.09375 to 0.09375
- dt_weight: bfloat16 [128, 4096], P(None, 'seq'), may hold values from -0.5 to 0.5
- dt_bias: bfloat16 [4096], P('seq'), may hold values from -6.91 to -2.25
- a_log: float32 [16, 4096], replicated, may hold values from -2.3 to 1.39
- skip_gain: float32 [4096], replicated, may hold values from 0.5 to 1.5
- out_weight: bfloat16 [4096, 2048], P('seq', 'req'), may hold values from -0.09375 to 0.09375
Outputs:
- mixed: bfloat16 [8, 2048, 2048], P('req', 'seq')
- final_state: float32 [8, 16, 4096], P('req', None, 'seq')
Inputs may be any that keep to these rules, and one draw needn't show every extreme that they name: `lengths`: each slot's length is at least 1, the longest is exactly 2048, and they sum to 10240. `slot_request`: A permutation of the requests.
All inputs are finite; a program needn't handle non-finite values.
Results may differ from a plain program's by a relative error of at most 0.015.
Values may be sent and summed in bfloat16 or wider, within the bound.
No kernel may reach another device: no remote copies, remote signals or barrier semaphores. Data moves between devices by JAX's collectives and lax.ppermute only.
A program may use at most 128 MiB of HBM per device.

v0:
```python
import jax
import jax.numpy as jnp
from jax import lax
from jax.sharding import PartitionSpec as P

STATE = 16
RANK = 128


def shifted(block, axis, distance):
    devices = range(lax.axis_size(axis))
    route = [(i - distance, i) for i in devices if i - distance in devices]
    return lax.ppermute(block, axis, route)


def spread(array, axis, root):
    mine = lax.axis_index(axis) == root
    return lax.psum(jnp.where(mine, array, jnp.zeros_like(array)), axis)


def to_blocks(array):
    pieces, length, columns = array.shape
    return jnp.moveaxis(array.reshape(pieces, 16, length // 16, columns), 1, 0)


def from_blocks(array):
    count, pieces, group, columns = array.shape
    return jnp.moveaxis(array, 0, 1).reshape(pieces, count * group, columns)


def piece_scan(rates, values, entry, readout, decay):
    pieces, length, columns = rates.shape
    group = length // 16
    positions = jnp.arange(length, dtype=jnp.int32)
    lower = (positions[None, :] <= positions[:, None]).astype(jnp.float32)
    running = jnp.einsum("rs,psw->prw", lower, rates, precision=lax.Precision.HIGHEST)

    def advance(state, items):
        rate, value, into, outof = items
        outputs = []
        for place in range(group):
            factor = jnp.exp(rate[:, place][:, None, :] * decay[None])
            state = (
                factor * state
                + (rate[:, place] * value[:, place])[:, None, :] * into[:, place][:, :, None]
            )
            outputs.append(jnp.sum(outof[:, place][:, :, None] * state, axis=1))
        return (state, jnp.stack(outputs, axis=1))

    start = jnp.zeros((pieces, decay.shape[0], columns), jnp.float32)
    end_local, local_out = lax.scan(
        advance, start, (to_blocks(rates), to_blocks(values), to_blocks(entry), to_blocks(readout))
    )
    total_decay = jnp.exp(running[:, length - 1][:, None, :] * decay[None])
    return (end_local, from_blocks(local_out), total_decay, running)


def carried_part(running, readout, decay, carry_in):

    def correct(items):
        total, outof = items
        kept = jnp.exp(total[:, :, None, :] * decay[None, None]) * carry_in[:, None]
        return jnp.sum(outof[:, :, :, None] * kept, axis=2)

    return from_blocks(lax.map(correct, (to_blocks(running), to_blocks(readout))))


def per_device(
    hidden,
    lengths,
    slot_request,
    norm_gain,
    in_weight,
    conv_weight,
    conv_bias,
    xproj_weight,
    dt_weight,
    dt_bias,
    a_log,
    skip_gain,
    out_weight,
):
    seq_count = lax.axis_size("seq")
    seq_index = lax.axis_index("seq")
    req_index = lax.axis_index("req")
    rows = hidden.shape[1]
    span = rows * seq_count
    width = in_weight.shape[2]
    taps_count = conv_weight.shape[0]
    state_count = a_log.shape[0]
    total_inner = a_log.shape[1]
    tokens = hidden[0].astype(jnp.float32)
    scale = lax.rsqrt(jnp.mean(tokens * tokens, axis=-1, keepdims=True) + 1e-05)
    normed = (tokens * scale * norm_gain.astype(jnp.float32)).astype(jnp.bfloat16)
    w_in = lax.all_gather(in_weight, "req", axis=1, tiled=True)
    w_flat = jnp.concatenate((w_in[0], w_in[1]), axis=1)
    both = jnp.dot(
        lax.all_gather(normed, "seq", axis=0, tiled=True),
        w_flat,
        preferred_element_type=jnp.float32,
    )
    xin = both[:, :width]
    zgate = both[:, width:].astype(jnp.bfloat16)
    padded = jnp.pad(xin, ((taps_count - 1, 0), (0, 0)))
    taps = conv_weight.astype(jnp.float32)
    convolved = conv_bias.astype(jnp.float32) + jnp.zeros_like(xin)
    for tap in range(taps_count):
        convolved = convolved + taps[tap] * padded[tap : tap + span, :]
    inner = jax.nn.silu(convolved).astype(jnp.bfloat16)
    partial_proj = jnp.dot(inner, xproj_weight, preferred_element_type=jnp.float32)
    length_here = lax.dynamic_index_in_dim(lengths, req_index, 0, keepdims=False)
    summed = lax.psum(partial_proj, "seq")
    live_all = (jnp.arange(span, dtype=jnp.int32) < length_here).astype(jnp.float32)
    rate_low = summed[:, :RANK].astype(jnp.bfloat16)
    delta_ch = (
        jax.nn.softplus(
            jnp.dot(rate_low, dt_weight, preferred_element_type=jnp.float32)
            + dt_bias.astype(jnp.float32)
        )
        * live_all[:, None]
    )
    w_out = lax.all_gather(out_weight, "req", axis=1, tiled=True)
    inner_tok = lax.all_to_all(inner, "seq", split_axis=0, concat_axis=1, tiled=True)
    delta_tok = lax.all_to_all(
        delta_ch.astype(jnp.bfloat16), "seq", split_axis=0, concat_axis=1, tiled=True
    ).astype(delta_ch.dtype)
    own_proj = lax.dynamic_slice_in_dim(summed, seq_index * rows, rows, 0)
    decay = -jnp.exp(a_log)
    inner_f = inner_tok.astype(jnp.float32)
    entry = own_proj[None, :, RANK : RANK + STATE]
    readout = own_proj[None, :, RANK + STATE :]
    end_local, local_out, total_decay, running = piece_scan(
        delta_tok[None], inner_f[None], entry, readout, decay
    )
    zeros_state = jnp.zeros((state_count, total_inner), jnp.float32)

    def relay(turn, incoming):
        return shifted(total_decay[0] * incoming + end_local[0], "seq", 1)

    carry_in = lax.fori_loop(0, seq_count - 1, relay, zeros_state)
    carried = carried_part(running, readout, decay, carry_in[None])
    scanned = ((local_out + carried)[0] + skip_gain * inner_f).astype(jnp.bfloat16)
    last = spread(
        (total_decay[0] * carry_in + end_local[0]).astype(jnp.bfloat16), "seq", seq_count - 1
    ).astype(jnp.float32)
    mine = lax.dynamic_slice_in_dim(last, seq_index * width, width, 1)
    scanned_ch = lax.all_to_all(scanned, "seq", split_axis=1, concat_axis=0, tiled=True)
    gated_ch = (scanned_ch.astype(jnp.float32) * jax.nn.silu(zgate.astype(jnp.float32))).astype(
        jnp.bfloat16
    )
    branch = lax.psum_scatter(
        jnp.dot(gated_ch, w_out, preferred_element_type=jnp.float32).astype(jnp.bfloat16),
        "seq",
        scatter_dimension=0,
        tiled=True,
    ).astype(jnp.float32)
    slot_all = lax.all_gather(mine[None], "req", axis=0, tiled=True)
    picked = (slot_request == req_index).astype(jnp.float32)
    final_state = jnp.sum(picked[:, None, None] * slot_all, axis=0, keepdims=True)
    mixed = (tokens + branch).astype(jnp.bfloat16)[None]
    return (mixed, final_state)


def solution(mesh):
    in_specs = (
        P("req", "seq", None),
        P(),
        P(),
        P(),
        P(None, "req", "seq"),
        P(None, "seq"),
        P("seq"),
        P("seq", None),
        P(None, "seq"),
        P("seq"),
        P(),
        P(),
        P("seq", "req"),
    )
    out_specs = (P("req", "seq", None), P("req", None, "seq"))
    return jax.shard_map(
        per_device, mesh=mesh, in_specs=in_specs, out_specs=out_specs, check_vma=False
    )
```

profile of v0, /device:TPU:0, one launch (start us, length us, event | category | flops | bytes accessed | tf_op | source)
XLA Modules:
  0.0 717.7 jit_solution(14593859675135900258)
XLA Ops:
  12.1 25.4 %all-gather.7.cloned.1.call-done = bf16[2,2048,256]{2,1,0:T(8,128)(2,1)} async-done(((bf16[2,256,256]{2,1,0:T(8,128)(2,1)}), bf16[2,2048,256]{2,1,0:T(8,128)(2,1)}) %all-gather.7.cloned.1.call-update) | async-done | bytes 2097168 | tf_op jit(solution)/shard_map/all_gather | solution.py:95
  39.2 72.3 %all-gather.5.cloned.1.call-done = bf16[2048,2048]{1,0:T(8,128)(2,1)} async-done(((bf16[128,2048]{1,0:T(8,128)(2,1)}), bf16[2048,2048]{1,0:T(8,128)(2,1)}) %all-gather.5.cloned.1.call-update) | async-done | bytes 8388624 | tf_op jit(solution)/shard_map/all_gather | solution.py:98
  111.5 6.9 fusion.33
  132.2 88.7 %all-reduce.4.cloned.1.call-done = f32[2048,160]{0,1:T(8,128)} async-done(((f32[2048,160]{0,1:T(8,128)}), f32[2048,160]{0,1:T(8,128)}) %all-reduce.4.cloned.1.call-update) | async-done | bytes 1310736 | tf_op jit(solution)/shard_map/psum | solution.py:112
  238.4 7.5 %all-to-all-done = bf16[16,128,256]{1,2,0:T(8,128)(2,1)S(1)} async-done(((bf16[16,128,256]{1,2,0:T(8,128)(2,1)}), bf16[16,128,256]{1,2,0:T(8,128)(2,1)S(1)}, u32[]{:S(2)}, u32[]{:S(2)}) %all-to-all-start) | async-done | bytes 1048608 | tf_op jit(solution)/shard_map/all_to_all | solution.py:124
  255.7 65.7 %while.35 = (s32[]{:T(128)}, f32[1,16,4096]{2,1,0:T(8,128)S(1)}, f32[16,1,8,4096]{3,2,1,0:T(8,128)}, f32[16,1,8,4096]{3,2,1,0:T(8,128)}, f32[16,4096]{1,0:T(8,12...) while((s32[]{:T(128)}, f32[1,16,4096]{2,1,0:T(8,128)S(1)}, ...), condition=%wide.region_11.12_spmd.clone, body=%wide.region_2.11_spmd.clone.sunk | while | flops 4849667 | bytes 4347896 | solution.py:51
  321.5 148.6 %while.33 = (s32[]{:T(128)}, f32[16,4096]{1,0:T(8,128)S(1)}, f32[1,16,4096]{2,1,0:T(8,128)S(1)}, f32[1,16,4096]{2,1,0:T(8,128)S(1)}, s32[]{:T(128)}) while((s32[]{:T(128)}, f32[16,4096]{1,0:T(8,128)S(1)}, f32[1,16,4096]{2,1,0:T(8,128)S(1)}, f32[1,16,4096]{2,1,0:T(8,128)S(1)}, s32[]{:T(128)}) %tuple.124), condition=%wide.region_13.14_spmd, body=%wide.region_12.13_spmd.sunk | while | flops 131074 | bytes 2097253 | solution.py:140
  341.8 6.1 collective-permute-done
  352.4 6.1 collective-permute-done
  385.2 6.8 collective-permute-start
  392.1 5.6 collective-permute-done
  397.7 6.2 collective-permute-start
  418.0 6.5 collective-permute-start
  428.4 6.5 collective-permute-start
  438.9 6.5 collective-permute-start
  449.3 6.5 collective-permute-start
  459.7 6.5 collective-permute-start
  471.6 35.8 %while.34 = (s32[]{:T(128)}, f32[16,1,8,4096]{3,2,1,0:T(8,128)}, f32[16,1,8,16]{3,2,1,0:T(8,128)S(1)}, f32[16,1,8,4096]{3,2,1,0:T(8,128)}, f32[16,4096]{1,0:T(8,128)S(1)}, /*index=5*/f32[16,4096]{1,0:T(8,128)S(1)}, s32[]{:T(128)}) while((s32[]{:T(128)}, f32[16,1,8,4096]{3,2,1,0:T(8,128)}, f32[16,1,8,16]{3,2,1,0:T(8,128)S(1)}, ...), condition=%wide.region_16.17_spmd, body=%wide.region_14.16_spmd.sunk | while | flops 2064386 | bytes 1312853 | solution.py:65
  512.9 18.0 %all-to-all-start.2 = ((bf16[128,16,256]{2,0,1:T(8,128)(2,1)}), bf16[128,16,256]{2,0,1:T(8,128)(2,1)S(1)}, u32[]{:S(2)}, u32[]{:S(2)}) async-start(bf16[128,16,256]{2,0,1:T(8,128)(2,1)} %fusion.30), calls=%async_computation.2 | async-start | bytes 2097152 | tf_op jit(solution)/shard_map/all_to_all | solution.py:147
  532.1 12.2 %all-to-all-done.2 = bf16[128,16,256]{2,0,1:T(8,128)(2,1)S(1)} async-done(((bf16[128,16,256]{2,0,1:T(8,128)(2,1)}), bf16[128,16,256]{2,0,1:T(8,128)(2,1)S(1)}, u32[]{:S(2)}, u32[]{:S(2)}) %all-to-all-start.2) | async-done | bytes 1048608 | tf_op jit(solution)/shard_map/all_to_all | solution.py:147
  546.7 6.8 convolution_convert_fusion
  554.1 66.1 %all-reduce.6.cloned.1.call-done = bf16[16,4096]{1,0:T(8,128)(2,1)} async-done(((bf16[16,4096]{1,0:T(8,128)(2,1)}), bf16[16,4096]{1,0:T(8,128)(2,1)}) %all-reduce.6.cloned.1.call-update) | async-done | bytes 131088 | tf_op jit(solution)/shard_map/psum | solution.py:18
  620.9 13.0 %all-gather = f32[128,256]{1,0:T(8,128)S(1)} all-gather(f32[16,256]{1,0:T(8,128)S(1)} %dynamic-slice_convert_fusion), channel_id=2, replica_groups=mesh['req'=8,'seq'=16] {'req'}, dimensions={0}, use_global_device_ids=true | all-gather | bytes 147456 | tf_op jit(solution)/shard_map/all_gather | solution.py:157
  634.6 74.3 %reduce-scatter.2.cloned.1.call-done = bf16[128,2048]{1,0:T(8,128)(2,1)} async-done(((bf16[2048,2048]{1,0:T(8,128)(2,1)}), bf16[128,2048]{1,0:T(8,128)(2,1)}) %reduce-scatter.2.cloned.1.call-update) | async-done | bytes 524304 | tf_op jit(solution)/shard_map/reduce_scatter | solution.py:151
  (364 shorter events, 247.2 us)
Async XLA Ops:
  7.2 30.3 %all-gather.7.cloned.1.call-start = ((), (), s32[]{:S(2)}) async-start(), calls=%async_computation.5 | async-start | bytes 2359296 | tf_op jit(solution)/shard_map/all_gather | solution.py:95
  7.9 103.6 %all-gather.5.cloned.1.call-start = ((), (), s32[]{:S(2)}) async-start(), calls=%async_computation.4 | async-start | bytes 8912896 | tf_op jit(solution)/shard_map/all_gather | solution.py:98
  12.0 209.0 %all-reduce.4.cloned.1.call-start = ((), (), s32[]{:S(2)}) async-start(), calls=%async_computation.6 | async-start | bytes 2621440 | tf_op jit(solution)/shard_map/psum | solution.py:112
  125.5 99.5 %all-to-all-start.1 = ((bf16[16,128,256]{2,1,0:T(8,128)(2,1)}), bf16[16,128,256]{2,1,0:T(8,128)(2,1)S(1)}, u32[]{:S(2)}, u32[]{:S(2)}) async-start(bf16[16,128,256]{2,1,0:T(8,128)(2,1)} %bitcast.17), calls=%async_computation.1 | async-start | bytes 2097152 | tf_op jit(solution)/shard_map/all_to_all | solution.py:123
  225.0 20.9 %all-to-all-start = ((bf16[16,128,256]{1,2,0:T(8,128)(2,1)}), bf16[16,128,256]{1,2,0:T(8,128)(2,1)S(1)}, u32[]{:S(2)}, u32[]{:S(2)}) async-start(bf16[16,128,256]{1,2,0:T(8,128)(2,1)} %copy.43), calls=%async_computation | async-start | bytes 2097152 | tf_op jit(solution)/shard_map/all_to_all | solution.py:124
  230.1 316.6 %all-gather.9.cloned.1.call-start = ((), (), s32[]{:S(2)}) async-start(), calls=%async_computation.7 | async-start | bytes 1179648 | tf_op jit(solution)/shard_map/all_gather | solution.py:122
  321.5 6.4 collective-permute-start
  328.0 9.4 %collective-permute-start = (f32[16,4096]{1,0:T(8,128)S(1)}, f32[16,4096]{1,0:T(8,128)S(1)}, u32[]{:S(2)}, u32[]{:S(2)}) collective-permute-start(f32[16,4096]{1,0:T(8,128)S(1)} %bitcast_add_fusion.3), channel_id=1, source_target_pairs={{0,1},{1,2},{2,3},{3,4},{4,5},{5,6},{6,7},{7,8},{8,9},{9,10},{10,1... | collective-permute-start | bytes 786440 | tf_op jit(solution)/shard_map/while/body/eval_jaxpr/ppermute | solution.py:13
  337.4 10.5 %collective-permute-start = (f32[16,4096]{1,0:T(8,128)S(1)}, f32[16,4096]{1,0:T(8,128)S(1)}, u32[]{:S(2)}, u32[]{:S(2)}) collective-permute-start(f32[16,4096]{1,0:T(8,128)S(1)} %bitcast_add_fusion.3), channel_id=1, source_target_pairs={{0,1},{1,2},{2,3},{3,4},{4,5},{5,6},{6,7},{7,8},{8,9},{9,10},{10,1... | collective-permute-start | bytes 786440 | tf_op jit(solution)/shard_map/while/body/eval_jaxpr/ppermute | solution.py:13
  347.9 10.5 %collective-permute-start = (f32[16,4096]{1,0:T(8,128)S(1)}, f32[16,4096]{1,0:T(8,128)S(1)}, u32[]{:S(2)}, u32[]{:S(2)}) collective-permute-start(f32[16,4096]{1,0:T(8,128)S(1)} %bitcast_add_fusion.3), channel_id=1, source_target_pairs={{0,1},{1,2},{2,3},{3,4},{4,5},{5,6},{6,7},{7,8},{8,9},{9,10},{10,1... | collective-permute-start | bytes 786440 | tf_op jit(solution)/shard_map/while/body/eval_jaxpr/ppermute | solution.py:13
  358.5 9.6 %collective-permute-start = (f32[16,4096]{1,0:T(8,128)S(1)}, f32[16,4096]{1,0:T(8,128)S(1)}, u32[]{:S(2)}, u32[]{:S(2)}) collective-permute-start(f32[16,4096]{1,0:T(8,128)S(1)} %bitcast_add_fusion.3), channel_id=1, source_target_pairs={{0,1},{1,2},{2,3},{3,4},{4,5},{5,6},{6,7},{7,8},{8,9},{9,10},{10,1... | collective-permute-start | bytes 786440 | tf_op jit(solution)/shard_map/while/body/eval_jaxpr/ppermute | solution.py:13
  368.1 8.8 %collective-permute-start = (f32[16,4096]{1,0:T(8,128)S(1)}, f32[16,4096]{1,0:T(8,128)S(1)}, u32[]{:S(2)}, u32[]{:S(2)}) collective-permute-start(f32[16,4096]{1,0:T(8,128)S(1)} %bitcast_add_fusion.3), channel_id=1, source_target_pairs={{0,1},{1,2},{2,3},{3,4},{4,5},{5,6},{6,7},{7,8},{8,9},{9,10},{10,1... | collective-permute-start | bytes 786440 | tf_op jit(solution)/shard_map/while/body/eval_jaxpr/ppermute | solution.py:13
  376.9 8.3 %collective-permute-start = (f32[16,4096]{1,0:T(8,128)S(1)}, f32[16,4096]{1,0:T(8,128)S(1)}, u32[]{:S(2)}, u32[]{:S(2)}) collective-permute-start(f32[16,4096]{1,0:T(8,128)S(1)} %bitcast_add_fusion.3), channel_id=1, source_target_pairs={{0,1},{1,2},{2,3},{3,4},{4,5},{5,6},{6,7},{7,8},{8,9},{9,10},{10,1... | collective-permute-start | bytes 786440 | tf_op jit(solution)/shard_map/while/body/eval_jaxpr/ppermute | solution.py:13
  385.2 12.5 %collective-permute-start = (f32[16,4096]{1,0:T(8,128)S(1)}, f32[16,4096]{1,0:T(8,128)S(1)}, u32[]{:S(2)}, u32[]{:S(2)}) collective-permute-start(f32[16,4096]{1,0:T(8,128)S(1)} %bitcast_add_fusion.3), channel_id=1, source_target_pairs={{0,1},{1,2},{2,3},{3,4},{4,5},{5,6},{6,7},{7,8},{8,9},{9,10},{10,1... | collective-permute-start | bytes 786440 | tf_op jit(solution)/shard_map/while/body/eval_jaxpr/ppermute | solution.py:13
  397.7 10.7 %collective-permute-start = (f32[16,4096]{1,0:T(8,128)S(1)}, f32[16,4096]{1,0:T(8,128)S(1)}, u32[]{:S(2)}, u32[]{:S(2)}) collective-permute-start(f32[16,4096]{1,0:T(8,128)S(1)} %bitcast_add_fusion.3), channel_id=1, source_target_pairs={{0,1},{1,2},{2,3},{3,4},{4,5},{5,6},{6,7},{7,8},{8,9},{9,10},{10,1... | collective-permute-start | bytes 786440 | tf_op jit(solution)/shard_map/while/body/eval_jaxpr/ppermute | solution.py:13
  408.5 9.5 %collective-permute-start = (f32[16,4096]{1,0:T(8,128)S(1)}, f32[16,4096]{1,0:T(8,128)S(1)}, u32[]{:S(2)}, u32[]{:S(2)}) collective-permute-start(f32[16,4096]{1,0:T(8,128)S(1)} %bitcast_add_fusion.3), channel_id=1, source_target_pairs={{0,1},{1,2},{2,3},{3,4},{4,5},{5,6},{6,7},{7,8},{8,9},{9,10},{10,1... | collective-permute-start | bytes 786440 | tf_op jit(solution)/shard_map/while/body/eval_jaxpr/ppermute | solution.py:13
  418.0 10.4 %collective-permute-start = (f32[16,4096]{1,0:T(8,128)S(1)}, f32[16,4096]{1,0:T(8,128)S(1)}, u32[]{:S(2)}, u32[]{:S(2)}) collective-permute-start(f32[16,4096]{1,0:T(8,128)S(1)} %bitcast_add_fusion.3), channel_id=1, source_target_pairs={{0,1},{1,2},{2,3},{3,4},{4,5},{5,6},{6,7},{7,8},{8,9},{9,10},{10,1... | collective-permute-start | bytes 786440 | tf_op jit(solution)/shard_map/while/body/eval_jaxpr/ppermute | solution.py:13
  428.4 10.4 %collective-permute-start = (f32[16,4096]{1,0:T(8,128)S(1)}, f32[16,4096]{1,0:T(8,128)S(1)}, u32[]{:S(2)}, u32[]{:S(2)}) collective-permute-start(f32[16,4096]{1,0:T(8,128)S(1)} %bitcast_add_fusion.3), channel_id=1, source_target_pairs={{0,1},{1,2},{2,3},{3,4},{4,5},{5,6},{6,7},{7,8},{8,9},{9,10},{10,1... | collective-permute-start | bytes 786440 | tf_op jit(solution)/shard_map/while/body/eval_jaxpr/ppermute | solution.py:13
  438.9 10.4 %collective-permute-start = (f32[16,4096]{1,0:T(8,128)S(1)}, f32[16,4096]{1,0:T(8,128)S(1)}, u32[]{:S(2)}, u32[]{:S(2)}) collective-permute-start(f32[16,4096]{1,0:T(8,128)S(1)} %bitcast_add_fusion.3), channel_id=1, source_target_pairs={{0,1},{1,2},{2,3},{3,4},{4,5},{5,6},{6,7},{7,8},{8,9},{9,10},{10,1... | collective-permute-start | bytes 786440 | tf_op jit(solution)/shard_map/while/body/eval_jaxpr/ppermute | solution.py:13
  449.3 10.4 %collective-permute-start = (f32[16,4096]{1,0:T(8,128)S(1)}, f32[16,4096]{1,0:T(8,128)S(1)}, u32[]{:S(2)}, u32[]{:S(2)}) collective-permute-start(f32[16,4096]{1,0:T(8,128)S(1)} %bitcast_add_fusion.3), channel_id=1, source_target_pairs={{0,1},{1,2},{2,3},{3,4},{4,5},{5,6},{6,7},{7,8},{8,9},{9,10},{10,1... | collective-permute-start | bytes 786440 | tf_op jit(solution)/shard_map/while/body/eval_jaxpr/ppermute | solution.py:13
  459.7 10.4 %collective-permute-start = (f32[16,4096]{1,0:T(8,128)S(1)}, f32[16,4096]{1,0:T(8,128)S(1)}, u32[]{:S(2)}, u32[]{:S(2)}) collective-permute-start(f32[16,4096]{1,0:T(8,128)S(1)} %bitcast_add_fusion.3), channel_id=1, source_target_pairs={{0,1},{1,2},{2,3},{3,4},{4,5},{5,6},{6,7},{7,8},{8,9},{9,10},{10,1... | collective-permute-start | bytes 786440 | tf_op jit(solution)/shard_map/while/body/eval_jaxpr/ppermute | solution.py:13
  512.9 31.4 %all-to-all-start.2 = ((bf16[128,16,256]{2,0,1:T(8,128)(2,1)}), bf16[128,16,256]{2,0,1:T(8,128)(2,1)S(1)}, u32[]{:S(2)}, u32[]{:S(2)}) async-start(bf16[128,16,256]{2,0,1:T(8,128)(2,1)} %fusion.30), calls=%async_computation.2 | async-start | bytes 2097152 | tf_op jit(solution)/shard_map/all_to_all | solution.py:147
  531.0 89.2 %all-reduce.6.cloned.1.call-start = ((), (), s32[]{:S(2)}) async-start(), calls=%async_computation.9 | async-start | bytes 262144 | tf_op jit(solution)/shard_map/psum | solution.py:18
  531.8 177.1 %reduce-scatter.2.cloned.1.call-start = ((), (), s32[]{:S(2)}) async-start(), calls=%async_computation.8 | async-start | bytes 8912896 | tf_op jit(solution)/shard_map/reduce_scatter | solution.py:151
  (16 other events, 597.8 us)
Sparse Core Ops, SparseCore 0:
  9.7 27.7 all-gather.6
  40.2 71.2 all-gather.4
  125.6 95.2 all-reduce.3
  232.3 24.7 all-gather.8
  535.2 84.9 all-reduce.5
  623.5 85.3 reduce-scatter.1
where the time goes:
time: 720 us; the launch traced here: 718 us
  waiting for transfers between devices  415 us (58%)
  starting transfers between devices  109 us (15%)
  local copies, waits for them, and re-layouts  89.9 us (12%)
  other arithmetic  54.7 us (8%)
  matrix products  19.6 us (3%)
  between operations  14.4 us (2%)
  blocking collectives  13 us (2%)
    psum x1, waiting for transfers between devices, per_device(): summed = lax.psum(partial_proj, 'seq')  88.7 us
    ppermute x15, starting transfers between devices, shifted(): return lax.ppermute(block, axis, route)  80.1 us
    reduce_scatter x1, waiting for transfers between devices, per_device(): lax.psum_scatter(jnp.dot(gated_ch, w_out, preferred_element_type=jnp.floa...  74.3 us
    all_gather x1, waiting for transfers between devices, per_device(): lax.all_gather(normed, 'seq', axis=0, tiled=True)  72.3 us
    ppermute x15, waiting for transfers between devices, shifted(): return lax.ppermute(block, axis, route)  67.6 us
    psum x1, waiting for transfers between devices, spread(): return lax.psum(jnp.where(mine, array, jnp.zeros_like(array)), axis)  66.1 us
    squeeze x32, local copies, waits for them, and re-layouts, piece_scan(): lax.scan(advance, start, (to_blocks(rates), to_blocks(values), to_blocks(...  26.9 us
    all_gather x1, waiting for transfers between devices, per_device(): w_in = lax.all_gather(in_weight, 'req', axis=1, tiled=True)  25.4 us
  transfers between devices with their start and end apart: 24, of which 22 were waited for; matrix products, arithmetic and copies ran while one was open for 20% of the time, Pallas kernels for 0%

commit v1 on v0

--- a/solution.py
+++ b/solution.py
@@ -5,6 +5,14 @@
 
 STATE = 16
 RANK = 128
+
+
+def leaves_play(block_here, at_axis):
+    block_here = jnp.moveaxis(block_here, 0, at_axis)
+    then = block_here.shape
+    return block_here.reshape(
+        *then[:at_axis], then[at_axis] * then[at_axis + 1], *then[at_axis + 2 :]
+    )
 
 
 def shifted(block, axis, distance):
@@ -92,7 +100,23 @@
     tokens = hidden[0].astype(jnp.float32)
     scale = lax.rsqrt(jnp.mean(tokens * tokens, axis=-1, keepdims=True) + 1e-05)
     normed = (tokens * scale * norm_gain.astype(jnp.float32)).astype(jnp.bfloat16)
-    w_in = lax.all_gather(in_weight, "req", axis=1, tiled=True)
+    q_n = lax.psum(1, axis_name="req")
+    so_far_all = [(t, (t + 1) % q_n) for t in range(q_n)]
+    local_next, even = ([], [])
+    fields = [(b, jj) for jj, b in so_far_all]
+    for dev_j in tuple(range(q_n - 1)):
+        if dev_j % 2 == 0:
+            local_next.append(
+                lax.ppermute(
+                    local_next[-1] if local_next else in_weight, axis_name="req", perm=so_far_all
+                )
+            )
+        else:
+            even.append(lax.ppermute(even[-1] if even else in_weight, axis_name="req", perm=fields))
+    out_arr = jnp.stack([*local_next[::-1], in_weight, *even])
+    z = lax.axis_index("req") - len(local_next)
+    out_arr = out_arr[(jnp.arange(q_n) - z) % q_n]
+    w_in = leaves_play(out_arr, 1)
     w_flat = jnp.concatenate((w_in[0], w_in[1]), axis=1)
     both = jnp.dot(
         lax.all_gather(normed, "seq", axis=0, tiled=True),

time: 720 us -> 696 us (0.967)
  waiting for transfers between devices: 415 us -> 372 us
  starting transfers between devices: 109 us -> 118 us
  local copies, waits for them, and re-layouts: 89.9 us -> 97.8 us
    all_gather x1, waiting for transfers between devices: 72.3 us -> 36.2 us  [per_device(): lax.all_gather(normed, 'seq', axis=0, tiled=True)]
    all_gather x1 -> x0, waiting for transfers between devices: 25.4 us -> none  [per_device(): w_in = lax.all_gather(in_weight, 'req', axis=1, tiled=True)]
    ppermute x0 -> x7, waiting for transfers between devices: none -> 19.1 us  [the longest x4 19 us: per_device(): lax.ppermute(local_next[-1] if local_next else in_weight, axis_name='req'...]
    ppermute x0 -> x7, starting transfers between devices: none -> 8.9 us  [the longest x3 8.87 us: per_device(): lax.ppermute(even[-1] if even else in_weight, axis_name='req', perm=fields)]
  transfers between devices with their start and end apart: 24 -> 30, of which waited for: 22 -> 25; matrix products, arithmetic and copies ran while one was open for 20% -> 22% of each run, Pallas kernels for 0% -> 0%
where the time goes in v1:
time: 696 us; the launch traced here: 693 us
  waiting for transfers between devices  372 us (53%)
  starting transfers between devices  118 us (17%)
  local copies, waits for them, and re-layouts  97.8 us (14%)
  other arithmetic  54.8 us (8%)
  matrix products  20 us (3%)
  between operations  15.6 us (2%)
  blocking collectives  13 us (2%)
    psum x1, waiting for transfers between devices, per_device(): summed = lax.psum(partial_proj, 'seq')  88.7 us
    ppermute x15, starting transfers between devices, shifted(): return lax.ppermute(block, axis, route)  80.2 us
    reduce_scatter x1, waiting for transfers between devices, per_device(): lax.psum_scatter(jnp.dot(gated_ch, w_out, preferred_element_type=jnp.floa...  74.3 us
    ppermute x15, waiting for transfers between devices, shifted(): return lax.ppermute(block, axis, route)  67.6 us
    psum x1, waiting for transfers between devices, spread(): return lax.psum(jnp.where(mine, array, jnp.zeros_like(array)), axis)  66.3 us
    all_gather x1, waiting for transfers between devices, per_device(): lax.all_gather(normed, 'seq', axis=0, tiled=True)  36.2 us
    squeeze x32, local copies, waits for them, and re-layouts, piece_scan(): lax.scan(advance, start, (to_blocks(rates), to_blocks(values), to_blocks(...  26.9 us
    dynamic_update_slice x32, local copies, waits for them, and re-layouts, piece_scan(): lax.scan(advance, start, (to_blocks(rates), to_blocks(values), to_blocks(...  21.4 us
  transfers between devices with their start and end apart: 30, of which 25 were waited for; matrix products, arithmetic and copies ran while one was open for 22% of the time, Pallas kernels for 0%

profile of v1, /device:TPU:0, one launch (start us, length us, event | category | flops | bytes accessed | tf_op | source)
XLA Modules:
  0.0 693.2 jit_solution(18442348756006711923)
XLA Ops:
  12.2 7.0 %collective-permute-done.1 = bf16[2,256,256]{2,1,0:T(8,128)(2,1)S(1)} collective-permute-done((bf16[2,256,256]{2,1,0:T(8,128)(2,1)S(1)}, bf16[2,256,256]{2,1,0:T(8,128)(2,1)S(1)}, u32[]{:S(2)}, u32[]{:S(2)}) %collective-permute-start.1) | collective-permute-done | bytes 262176 | tf_op jit(solution)/shard_map/ppermute | solution.py:110
  49.6 36.2 %all-gather.4.cloned.1.call-done = bf16[2048,2048]{1,0:T(8,128)(2,1)} async-done(((bf16[128,2048]{1,0:T(8,128)(2,1)}), bf16[2048,2048]{1,0:T(8,128)(2,1)}) %all-gather.4.cloned.1.call-update) | async-done | bytes 8388624 | tf_op jit(solution)/shard_map/all_gather | solution.py:122
  85.7 7.2 %fusion.33 = f32[2048,512]{1,0:T(8,128)S(1)} fusion(bf16[2048,2048]{1,0:T(8,128)(2,1)} %all-gather.4.cloned.1.call-done, bf16[2048,256]{1,0:T(8,128)(2,1)} %bitcast.374, bf16[2048,256]{1,0:T(8,128)(2,1)S(1)} %bitcast.373), kind=kOutput, calls=%fused_computation.93 | convolution fusion | flops 4299161600 | bytes 14680064 | tf_op jit(solution)/shard_map/dot_general | solution.py:121
  106.8 88.7 %all-reduce.4.cloned.1.call-done = f32[2048,160]{0,1:T(8,128)} async-done(((f32[2048,160]{0,1:T(8,128)}), f32[2048,160]{0,1:T(8,128)}) %all-reduce.4.cloned.1.call-update) | async-done | bytes 1310736 | tf_op jit(solution)/shard_map/psum | solution.py:136
  213.0 7.5 %all-to-all-done = bf16[16,128,256]{1,2,0:T(8,128)(2,1)S(1)} async-done(((bf16[16,128,256]{1,2,0:T(8,128)(2,1)}), bf16[16,128,256]{1,2,0:T(8,128)(2,1)S(1)}, u32[]{:S(2)}, u32[]{:S(2)}) %all-to-all-start) | async-done | bytes 1048608 | tf_op jit(solution)/shard_map/all_to_all | solution.py:148
  230.3 65.8 %while.35 = (s32[]{:T(128)}, f32[1,16,4096]{2,1,0:T(8,128)S(1)}, f32[16,1,8,4096]{3,2,1,0:T(8,128)}, f32[16,1,8,4096]{3,2,1,0:T(8,128)}, f32[16,4096]{1,0:T(8,12...) while((s32[]{:T(128)}, f32[1,16,4096]{2,1,0:T(8,128)S(1)}, ...), condition=%wide.region_11.12_spmd.clone, body=%wide.region_2.11_spmd.clone.sunk | while | flops 4849667 | bytes 4347896 | solution.py:59
  296.1 148.6 %while.33 = (s32[]{:T(128)}, f32[16,4096]{1,0:T(8,128)S(1)}, f32[1,16,4096]{2,1,0:T(8,128)S(1)}, f32[1,16,4096]{2,1,0:T(8,128)S(1)}, s32[]{:T(128)}) while((s32[]{:T(128)}, f32[16,4096]{1,0:T(8,128)S(1)}, f32[1,16,4096]{2,1,0:T(8,128)S(1)}, f32[1,16,4096]{2,1,0:T(8,128)S(1)}, s32[]{:T(128)}) %tuple.124), condition=%wide.region_13.14_spmd, body=%wide.region_12.13_spmd.sunk | while | flops 131074 | bytes 2097253 | solution.py:164
  316.4 6.1 collective-permute-done
  326.9 6.1 collective-permute-done
  359.9 6.9 collective-permute-start
  372.4 6.2 collective-permute-start
  383.1 5.6 collective-permute-start
  392.7 6.5 collective-permute-start
  403.1 6.5 collective-permute-start
  413.5 6.5 collective-permute-start
  423.9 6.5 collective-permute-start
  434.3 6.5 collective-permute-start
  446.3 35.9 %while.34 = (s32[]{:T(128)}, f32[16,1,8,4096]{3,2,1,0:T(8,128)}, f32[16,1,8,16]{3,2,1,0:T(8,128)S(1)}, f32[16,1,8,4096]{3,2,1,0:T(8,128)}, f32[16,4096]{1,0:T(8,128)S(1)}, /*index=5*/f32[16,4096]{1,0:T(8,128)S(1)}, s32[]{:T(128)}) while((s32[]{:T(128)}, f32[16,1,8,4096]{3,2,1,0:T(8,128)}, f32[16,1,8,16]{3,2,1,0:T(8,128)S(1)}, ...), condition=%wide.region_16.17_spmd, body=%wide.region_14.16_spmd.sunk | while | flops 2064386 | bytes 1312853 | solution.py:73
  487.7 18.2 %all-to-all-start.2 = ((bf16[128,16,256]{2,0,1:T(8,128)(2,1)}), bf16[128,16,256]{2,0,1:T(8,128)(2,1)S(1)}, u32[]{:S(2)}, u32[]{:S(2)}) async-start(bf16[128,16,256]{2,0,1:T(8,128)(2,1)} %fusion.30), calls=%async_computation.2 | async-start | bytes 2097152 | tf_op jit(solution)/shard_map/all_to_all | solution.py:171
  507.0 12.2 %all-to-all-done.2 = bf16[128,16,256]{2,0,1:T(8,128)(2,1)S(1)} async-done(((bf16[128,16,256]{2,0,1:T(8,128)(2,1)}), bf16[128,16,256]{2,0,1:T(8,128)(2,1)S(1)}, u32[]{:S(2)}, u32[]{:S(2)}) %all-to-all-start.2) | async-done | bytes 1048608 | tf_op jit(solution)/shard_map/all_to_all | solution.py:171
  521.6 6.8 convolution_convert_fusion
  529.0 66.3 %all-reduce.6.cloned.1.call-done = bf16[16,4096]{1,0:T(8,128)(2,1)} async-done(((bf16[16,4096]{1,0:T(8,128)(2,1)}), bf16[16,4096]{1,0:T(8,128)(2,1)}) %all-reduce.6.cloned.1.call-update) | async-done | bytes 131088 | tf_op jit(solution)/shard_map/psum | solution.py:26
  596.1 13.0 %all-gather = f32[128,256]{1,0:T(8,128)S(1)} all-gather(f32[16,256]{1,0:T(8,128)S(1)} %dynamic-slice_convert_fusion), channel_id=2, replica_groups=mesh['req'=8,'seq'=16] {'req'}, dimensions={0}, use_global_device_ids=true | all-gather | bytes 147456 | tf_op jit(solution)/shard_map/all_gather | solution.py:181
  609.8 74.3 %reduce-scatter.2.cloned.1.call-done = bf16[128,2048]{1,0:T(8,128)(2,1)} async-done(((bf16[2048,2048]{1,0:T(8,128)(2,1)}), bf16[128,2048]{1,0:T(8,128)(2,1)}) %reduce-scatter.2.cloned.1.call-update) | async-done | bytes 524304 | tf_op jit(solution)/shard_map/reduce_scatter | solution.py:175
  (388 shorter events, 275.4 us)
Async XLA Ops:
  8.0 77.7 %all-gather.4.cloned.1.call-start = ((), (), s32[]{:S(2)}) async-start(), calls=%async_computation.4 | async-start | bytes 8912896 | tf_op jit(solution)/shard_map/all_gather | solution.py:122
  12.1 183.3 %all-reduce.4.cloned.1.call-start = ((), (), s32[]{:S(2)}) async-start(), calls=%async_computation.5 | async-start | bytes 2621440 | tf_op jit(solution)/shard_map/psum | solution.py:136
  26.2 7.0 %collective-permute-start.6 = (bf16[2,256,256]{2,1,0:T(8,128)(2,1)S(1)}, bf16[2,256,256]{2,1,0:T(8,128)(2,1)S(1)}, u32[]{:S(2)}, u32[]{:S(2)}) collective-permute-start(bf16[2,256,256]{2,1,0:T(8,128)(2,1)S(1)} %collective-permute-done.5), channel_id=1, source_target_pairs={{16,0},{32,16},{48,32},{64,48},{80,64},{96,80},{112,96},{0,112},{1... | collective-permute-start | bytes 786440 | tf_op jit(solution)/shard_map/ppermute | solution.py:115
  33.3 12.0 %collective-permute-start.7 = (bf16[2,256,256]{2,1,0:T(8,128)(2,1)S(1)}, bf16[2,256,256]{2,1,0:T(8,128)(2,1)S(1)}, u32[]{:S(2)}, u32[]{:S(2)}) collective-permute-start(bf16[2,256,256]{2,1,0:T(8,128)(2,1)S(1)} %collective-permute-done.6), channel_id=1, source_target_pairs={{16,0},{32,16},{48,32},{64,48},{80,64},{96,80},{112,96},{0,112},{1... | collective-permute-start | bytes 786440 | tf_op jit(solution)/shard_map/ppermute | solution.py:115
  100.1 99.5 %all-to-all-start.1 = ((bf16[16,128,256]{2,1,0:T(8,128)(2,1)}), bf16[16,128,256]{2,1,0:T(8,128)(2,1)S(1)}, u32[]{:S(2)}, u32[]{:S(2)}) async-start(bf16[16,128,256]{2,1,0:T(8,128)(2,1)} %bitcast.27), calls=%async_computation.1 | async-start | bytes 2097152 | tf_op jit(solution)/shard_map/all_to_all | solution.py:147
  199.5 20.9 %all-to-all-start = ((bf16[16,128,256]{1,2,0:T(8,128)(2,1)}), bf16[16,128,256]{1,2,0:T(8,128)(2,1)S(1)}, u32[]{:S(2)}, u32[]{:S(2)}) async-start(bf16[16,128,256]{1,2,0:T(8,128)(2,1)} %copy.43), calls=%async_computation | async-start | bytes 2097152 | tf_op jit(solution)/shard_map/all_to_all | solution.py:148
  204.6 316.9 %all-gather.6.cloned.1.call-start = ((), (), s32[]{:S(2)}) async-start(), calls=%async_computation.6 | async-start | bytes 1179648 | tf_op jit(solution)/shard_map/all_gather | solution.py:146
  302.6 9.4 %collective-permute-start = (f32[16,4096]{1,0:T(8,128)S(1)}, f32[16,4096]{1,0:T(8,128)S(1)}, u32[]{:S(2)}, u32[]{:S(2)}) collective-permute-start(f32[16,4096]{1,0:T(8,128)S(1)} %bitcast_add_fusion.3), channel_id=1, source_target_pairs={{0,1},{1,2},{2,3},{3,4},{4,5},{5,6},{6,7},{7,8},{8,9},{9,10},{10,1... | collective-permute-start | bytes 786440 | tf_op jit(solution)/shard_map/while/body/eval_jaxpr/ppermute | solution.py:21
  312.0 10.5 %collective-permute-start = (f32[16,4096]{1,0:T(8,128)S(1)}, f32[16,4096]{1,0:T(8,128)S(1)}, u32[]{:S(2)}, u32[]{:S(2)}) collective-permute-start(f32[16,4096]{1,0:T(8,128)S(1)} %bitcast_add_fusion.3), channel_id=1, source_target_pairs={{0,1},{1,2},{2,3},{3,4},{4,5},{5,6},{6,7},{7,8},{8,9},{9,10},{10,1... | collective-permute-start | bytes 786440 | tf_op jit(solution)/shard_map/while/body/eval_jaxpr/ppermute | solution.py:21
  322.5 10.5 %collective-permute-start = (f32[16,4096]{1,0:T(8,128)S(1)}, f32[16,4096]{1,0:T(8,128)S(1)}, u32[]{:S(2)}, u32[]{:S(2)}) collective-permute-start(f32[16,4096]{1,0:T(8,128)S(1)} %bitcast_add_fusion.3), channel_id=1, source_target_pairs={{0,1},{1,2},{2,3},{3,4},{4,5},{5,6},{6,7},{7,8},{8,9},{9,10},{10,1... | collective-permute-start | bytes 786440 | tf_op jit(solution)/shard_map/while/body/eval_jaxpr/ppermute | solution.py:21
  333.0 9.6 %collective-permute-start = (f32[16,4096]{1,0:T(8,128)S(1)}, f32[16,4096]{1,0:T(8,128)S(1)}, u32[]{:S(2)}, u32[]{:S(2)}) collective-permute-start(f32[16,4096]{1,0:T(8,128)S(1)} %bitcast_add_fusion.3), channel_id=1, source_target_pairs={{0,1},{1,2},{2,3},{3,4},{4,5},{5,6},{6,7},{7,8},{8,9},{9,10},{10,1... | collective-permute-start | bytes 786440 | tf_op jit(solution)/shard_map/while/body/eval_jaxpr/ppermute | solution.py:21
  342.7 8.8 %collective-permute-start = (f32[16,4096]{1,0:T(8,128)S(1)}, f32[16,4096]{1,0:T(8,128)S(1)}, u32[]{:S(2)}, u32[]{:S(2)}) collective-permute-start(f32[16,4096]{1,0:T(8,128)S(1)} %bitcast_add_fusion.3), channel_id=1, source_target_pairs={{0,1},{1,2},{2,3},{3,4},{4,5},{5,6},{6,7},{7,8},{8,9},{9,10},{10,1... | collective-permute-start | bytes 786440 | tf_op jit(solution)/shard_map/while/body/eval_jaxpr/ppermute | solution.py:21
  351.6 8.3 %collective-permute-start = (f32[16,4096]{1,0:T(8,128)S(1)}, f32[16,4096]{1,0:T(8,128)S(1)}, u32[]{:S(2)}, u32[]{:S(2)}) collective-permute-start(f32[16,4096]{1,0:T(8,128)S(1)} %bitcast_add_fusion.3), channel_id=1, source_target_pairs={{0,1},{1,2},{2,3},{3,4},{4,5},{5,6},{6,7},{7,8},{8,9},{9,10},{10,1... | collective-permute-start | bytes 786440 | tf_op jit(solution)/shard_map/while/body/eval_jaxpr/ppermute | solution.py:21
  359.9 12.5 %collective-permute-start = (f32[16,4096]{1,0:T(8,128)S(1)}, f32[16,4096]{1,0:T(8,128)S(1)}, u32[]{:S(2)}, u32[]{:S(2)}) collective-permute-start(f32[16,4096]{1,0:T(8,128)S(1)} %bitcast_add_fusion.3), channel_id=1, source_target_pairs={{0,1},{1,2},{2,3},{3,4},{4,5},{5,6},{6,7},{7,8},{8,9},{9,10},{10,1... | collective-permute-start | bytes 786440 | tf_op jit(solution)/shard_map/while/body/eval_jaxpr/ppermute | solution.py:21
  372.4 10.7 %collective-permute-start = (f32[16,4096]{1,0:T(8,128)S(1)}, f32[16,4096]{1,0:T(8,128)S(1)}, u32[]{:S(2)}, u32[]{:S(2)}) collective-permute-start(f32[16,4096]{1,0:T(8,128)S(1)} %bitcast_add_fusion.3), channel_id=1, source_target_pairs={{0,1},{1,2},{2,3},{3,4},{4,5},{5,6},{6,7},{7,8},{8,9},{9,10},{10,1... | collective-permute-start | bytes 786440 | tf_op jit(solution)/shard_map/while/body/eval_jaxpr/ppermute | solution.py:21
  383.1 9.5 %collective-permute-start = (f32[16,4096]{1,0:T(8,128)S(1)}, f32[16,4096]{1,0:T(8,128)S(1)}, u32[]{:S(2)}, u32[]{:S(2)}) collective-permute-start(f32[16,4096]{1,0:T(8,128)S(1)} %bitcast_add_fusion.3), channel_id=1, source_target_pairs={{0,1},{1,2},{2,3},{3,4},{4,5},{5,6},{6,7},{7,8},{8,9},{9,10},{10,1... | collective-permute-start | bytes 786440 | tf_op jit(solution)/shard_map/while/body/eval_jaxpr/ppermute | solution.py:21
  392.7 10.4 %collective-permute-start = (f32[16,4096]{1,0:T(8,128)S(1)}, f32[16,4096]{1,0:T(8,128)S(1)}, u32[]{:S(2)}, u32[]{:S(2)}) collective-permute-start(f32[16,4096]{1,0:T(8,128)S(1)} %bitcast_add_fusion.3), channel_id=1, source_target_pairs={{0,1},{1,2},{2,3},{3,4},{4,5},{5,6},{6,7},{7,8},{8,9},{9,10},{10,1... | collective-permute-start | bytes 786440 | tf_op jit(solution)/shard_map/while/body/eval_jaxpr/ppermute | solution.py:21
  403.1 10.4 %collective-permute-start = (f32[16,4096]{1,0:T(8,128)S(1)}, f32[16,4096]{1,0:T(8,128)S(1)}, u32[]{:S(2)}, u32[]{:S(2)}) collective-permute-start(f32[16,4096]{1,0:T(8,128)S(1)} %bitcast_add_fusion.3), channel_id=1, source_target_pairs={{0,1},{1,2},{2,3},{3,4},{4,5},{5,6},{6,7},{7,8},{8,9},{9,10},{10,1... | collective-permute-start | bytes 786440 | tf_op jit(solution)/shard_map/while/body/eval_jaxpr/ppermute | solution.py:21
  413.5 10.4 %collective-permute-start = (f32[16,4096]{1,0:T(8,128)S(1)}, f32[16,4096]{1,0:T(8,128)S(1)}, u32[]{:S(2)}, u32[]{:S(2)}) collective-permute-start(f32[16,4096]{1,0:T(8,128)S(1)} %bitcast_add_fusion.3), channel_id=1, source_target_pairs={{0,1},{1,2},{2,3},{3,4},{4,5},{5,6},{6,7},{7,8},{8,9},{9,10},{10,1... | collective-permute-start | bytes 786440 | tf_op jit(solution)/shard_map/while/body/eval_jaxpr/ppermute | solution.py:21
  423.9 10.4 %collective-permute-start = (f32[16,4096]{1,0:T(8,128)S(1)}, f32[16,4096]{1,0:T(8,128)S(1)}, u32[]{:S(2)}, u32[]{:S(2)}) collective-permute-start(f32[16,4096]{1,0:T(8,128)S(1)} %bitcast_add_fusion.3), channel_id=1, source_target_pairs={{0,1},{1,2},{2,3},{3,4},{4,5},{5,6},{6,7},{7,8},{8,9},{9,10},{10,1... | collective-permute-start | bytes 786440 | tf_op jit(solution)/shard_map/while/body/eval_jaxpr/ppermute | solution.py:21
  434.3 10.4 %collective-permute-start = (f32[16,4096]{1,0:T(8,128)S(1)}, f32[16,4096]{1,0:T(8,128)S(1)}, u32[]{:S(2)}, u32[]{:S(2)}) collective-permute-start(f32[16,4096]{1,0:T(8,128)S(1)} %bitcast_add_fusion.3), channel_id=1, source_target_pairs={{0,1},{1,2},{2,3},{3,4},{4,5},{5,6},{6,7},{7,8},{8,9},{9,10},{10,1... | collective-permute-start | bytes 786440 | tf_op jit(solution)/shard_map/while/body/eval_jaxpr/ppermute | solution.py:21
  487.7 31.5 %all-to-all-start.2 = ((bf16[128,16,256]{2,0,1:T(8,128)(2,1)}), bf16[128,16,256]{2,0,1:T(8,128)(2,1)S(1)}, u32[]{:S(2)}, u32[]{:S(2)}) async-start(bf16[128,16,256]{2,0,1:T(8,128)(2,1)} %fusion.30), calls=%async_computation.2 | async-start | bytes 2097152 | tf_op jit(solution)/shard_map/all_to_all | solution.py:171
  505.9 89.5 %all-reduce.6.cloned.1.call-start = ((), (), s32[]{:S(2)}) async-start(), calls=%async_computation.8 | async-start | bytes 262144 | tf_op jit(solution)/shard_map/psum | solution.py:26
  506.7 177.3 %reduce-scatter.2.cloned.1.call-start = ((), (), s32[]{:S(2)}) async-start(), calls=%async_computation.7 | async-start | bytes 8912896 | tf_op jit(solution)/shard_map/reduce_scatter | solution.py:175
  (23 other events, 658.6 us)
Sparse Core Ops, SparseCore 0:
  12.3 73.4 all-gather.3
  100.2 95.2 all-reduce.3
  510.5 84.8 all-reduce.5
  598.6 85.3 reduce-scatter.1
Sparse Core Ops, SparseCore 1:
  206.8 24.6 all-gather.5
